TPU v7x, 128 devices: a whole 4x4x4 slice. The times are simulated.
128 devices in a mesh: section: 2 (over core), seq: 4 (over x), tensor: 16 (over z, y).
Axes of the slice: x: 4, y: 4, z: 4, core: 2. Of those that a mesh axis runs over, the one named last changes fastest.
Arguments:
- queries: bfloat16 [2560, 8192], P(('section', 'seq'), 'tensor'), may hold values from -200 to 200
- neighbours: bfloat16 [10240, 8192], P(('section', 'seq', 'tensor')), may hold values from -6 to 6
- kv_weight: bfloat16 [2, 8192, 8192], P(None, None, 'tensor'), may hold values from -0.0625 to 0.0625
- out_weight: bfloat16 [8192, 8192], P('tensor'), may hold values from -0.5 to 0.5
- slot_map: int32 [40], replicated, may hold values from 0 to 39, as said below
Outputs:
- mixed: bfloat16 [2560, 8192], P(('section', 'seq', 'tensor'))
Inputs may be any that keep to these rules, and one draw needn't show every extreme that they name: `slot_map`: distinct numbers; slot s lies on encoder shard s // 5; at most 2 spans of one sequence shard map to one encoder shard, and that many do for some pair of shards.
All inputs are finite; a program needn't handle non-finite values.
Results may differ from a plain program's by a relative error of at most 0.013.
Values may be sent and summed in bfloat16 or wider, within the bound.
No kernel may reach another device: no remote copies, remote signals or barrier semaphores. Data moves between devices by JAX's collectives and lax.ppermute only.
A program may use at most 128 MiB of HBM per device.

v0:
```python
import math
import jax
import jax.numpy as jnp
from jax import lax
from jax.sharding import PartitionSpec as P

HD = 128
SPAN = 64
PEER = 2
CH_DEV = 5
CAPC = 5
KEYS = 256


def attend(query_block, key_values):
    scores = jnp.einsum(
        "bqhd,bkhd->bhqk", query_block, key_values[:, :, 0], preferred_element_type=jnp.float32
    )
    scores = scores * (1.0 / math.sqrt(HD))
    peak = jnp.max(scores, axis=-1, keepdims=True)
    expo = jnp.exp(scores - peak)
    weights = (expo / jnp.sum(expo, axis=-1, keepdims=True)).astype(jnp.bfloat16)
    result = jnp.einsum(
        "bhqk,bkhd->bqhd", weights, key_values[:, :, 1], preferred_element_type=jnp.float32
    )
    return result.astype(jnp.bfloat16)


def on_device(queries, neighbours, kv_weight, out_weight, slot_map):
    groups = lax.axis_size(("section", "seq"))
    group_index = lax.axis_index(("section", "seq"))
    heads_local = kv_weight.shape[2] // HD
    per_peer = PEER
    spans = slot_map.shape[0]
    row_block = lax.all_gather(neighbours, "tensor", axis=0, tiled=True)
    result = jnp.einsum("rd,kde->rke", row_block, kv_weight, preferred_element_type=jnp.float32)
    projected = result.astype(jnp.bfloat16).reshape(row_block.shape[0], 2 * kv_weight.shape[2])
    slot_values = projected.reshape(CAPC, KEYS, 2, heads_local, HD)
    span_ids = jnp.arange(spans, dtype=jnp.int32)
    owner_shard = slot_map // CAPC
    slot_index = slot_map % CAPC
    seq_owner = span_ids // CH_DEV
    earlier = (seq_owner[:, None] == seq_owner[None, :]) & (
        owner_shard[:, None] == owner_shard[None, :]
    )
    earlier = earlier & (span_ids[None, :] < span_ids[:, None])
    arrival = jnp.sum(earlier.astype(jnp.int32), axis=1)
    target_ids = jnp.arange(groups, dtype=jnp.int32)[:, None, None]
    place_ids = jnp.arange(per_peer, dtype=jnp.int32)[None, :, None]
    selection = (seq_owner[None, None, :] == target_ids) & (arrival[None, None, :] == place_ids)
    selection = selection & (owner_shard[None, None, :] == group_index)
    send_slot = jnp.sum(jnp.where(selection, slot_index[None, None, :], 0), axis=-1)
    occupied = jnp.any(selection, axis=-1)
    own_shards = lax.dynamic_slice_in_dim(owner_shard, group_index * CH_DEV, CH_DEV)
    own_arrival = lax.dynamic_slice_in_dim(arrival, group_index * CH_DEV, CH_DEV)
    own_place = own_shards * per_peer + own_arrival
    query_blocks = queries.reshape(CH_DEV, SPAN, heads_local, HD)
    local_pairs = jnp.where(
        occupied[:, :, None, None, None, None], slot_values[send_slot], jnp.zeros((), jnp.bfloat16)
    )
    received = lax.all_to_all(
        local_pairs, ("section", "seq"), split_axis=0, concat_axis=0, tiled=True
    )
    key_values = received.reshape(groups * per_peer, KEYS, 2, heads_local, HD)[own_place]
    attended = attend(query_blocks, key_values)
    attended_flat = attended.reshape(CH_DEV * SPAN, heads_local * HD)
    mixed = lax.psum_scatter(
        jnp.dot(attended_flat, out_weight, preferred_element_type=jnp.float32),
        "tensor",
        scatter_dimension=0,
        tiled=True,
    )
    return mixed.astype(jnp.bfloat16)


def solution(mesh):
    placed = (
        P(("section", "seq"), "tensor"),
        P(("section", "seq", "tensor"), None),
        P(None, None, "tensor"),
        P("tensor", None),
        P(),
    )
    return jax.shard_map(
        on_device,
        mesh=mesh,
        in_specs=placed,
        out_specs=P(("section", "seq", "tensor"), None),
        check_vma=False,
    )
```

profile of v0, /device:TPU:0, one launch (start us, length us, event | category | flops | bytes accessed | tf_op | source)
XLA Modules:
  0.0 552.6 jit_solution(7348434239065273170)
XLA Ops:
  6.5 0.0 all-gather.2.cloned.1.call-start
  6.5 0.7 all-gather.2.cloned.1.call-update
  7.3 0.7 broadcast_compare_fusion
  8.0 0.2 convert_reduce_fusion
  8.1 0.7 and_select_fusion
  8.8 0.1 select_reduce_fusion
  9.0 0.1 copy.21
  9.1 0.1 reshape.121
  9.1 0.2 fusion.18
  9.3 0.1 copy.20
  9.4 135.4 %all-gather.2.cloned.1.call-done = bf16[1280,8192]{1,0:T(8,128)(2,1)} async-done(((bf16[80,8192]{1,0:T(8,128)(2,1)}), bf16[1280,8192]{1,0:T(8,128)(2,1)}) %all-gather.2.cloned.1.call-update) | async-done | bytes 20971536 | tf_op jit(solution)/shard_map/all_gather | solution.py:35
  144.8 28.1 %fusion.3 = bf16[1280,2,512]{2,0,1:T(8,128)(2,1)} fusion(bf16[2,8192,512]{2,1,0:T(8,128)(2,1)} %param.7, bf16[1280,8192]{1,0:T(8,128)(2,1)} %all-gather.2.cloned.1.call-done), kind=kOutput, calls=%fused_computation.6 | convolution fusion | flops 21476147200 | bytes 40370176 | tf_op jit(solution)/shard_map/rd,kde->rke/dot_general | solution.py:36
  172.8 3.5 reshape_reshape.3
  176.4 8.8 %gather_fusion = bf16[16,256,2,4,128]{4,3,1,2,0:T(4,128)(2,1)} fusion(bf16[5,256,2,4,128]{4,3,1,0,2:T(4,128)(2,1)S(1)} %reshape_reshape.3, s32[1024]{0:T(1024)S(1)} %pad_clamp_fusion.1), kind=kCustom, calls=%fused_computation | custom fusion | bytes 16777280 | tf_op jit(solution)/shard_map/gather | solution.py:59
  185.2 7.7 %copy_select_fusion = bf16[8,2,256,2,4,128]{5,2,4,3,1,0:T(8,128)(2,1)} fusion(bf16[8,2,256,2,4,128]{5,4,2,3,1,0:T(4,128)(2,1)} %bitcast.41, pred[8,2]{1,0:T(8,128)(4,1)S(1)} %copy.20), kind=kLoop, calls=%fused_computation.5 | loop fusion | flops 4194304 | bytes 16777232 | tf_op jit(solution)/shard_map/jit(_where)/select_n | solution.py:58
  192.9 0.0 copy-start.1
  192.9 5.4 all-to-all-start
  198.3 0.0 copy-done.1
  198.3 0.1 reshape.117
  198.4 0.0 copy-done.2
  198.4 0.6 dynamic-slice
  199.6 0.1 compare_select_fusion.1
  199.7 92.3 %all-to-all-done = bf16[8,2,256,2,4,128]{5,2,4,3,1,0:T(8,128)(2,1)} async-done(((bf16[8,2,256,2,4,128]{5,2,4,3,1,0:T(8,128)(2,1)}), bf16[8,2,256,2,4,128]{5,2,4,3,1,0:T(8,128)(2,1)}, u32[]{:S(2)}, u32[]{:S(2)}) %all-to-all-start) | async-done | bytes 8388640 | tf_op jit(solution)/shard_map/all_to_all | solution.py:61
  292.0 4.4 gather_fusion.1
  296.4 0.6 fusion.8
  297.0 1.1 copy-done
  298.1 0.4 fusion.20
  298.5 4.0 fusion.11
  302.6 0.3 copy.26
  302.8 8.9 %fusion.13 = f32[320,8192]{1,0:T(8,128)} fusion(bf16[512,8192]{1,0:T(8,128)(2,1)} %param.8, bf16[40,8,4,128]{3,2,1,0:T(4,128)(2,1)S(1)} %bitcast.42), kind=kOutput, calls=%fused_computation.19 | convolution fusion | flops 2684354560 | bytes 19202048 | tf_op jit(solution)/shard_map/dot_general | solution.py:68
  311.8 232.1 %all-reduce.2 = bf16[320,8192]{1,0:T(8,128)(2,1)} all-reduce(f32[320,8192]{1,0:T(8,128)} %fusion.13), channel_id=2, replica_groups=mesh['section'=2,'seq'=4,'tensor'=16] {'tensor'}, use_global_device_ids=true, to_apply=%region_5.6.clone | all-reduce | flops 2621440 | bytes 15728640
  543.9 1.9 dynamic-slice_convert_fusion
  (8 shorter events, 0.0 us)
Async XLA Ops:
  6.5 138.2 %all-gather.2.cloned.1.call-start = ((), (), s32[]{:S(2)}) async-start(), calls=%async_computation.1 | async-start | bytes 22282240 | tf_op jit(solution)/shard_map/all_gather | solution.py:35
  192.9 5.4 copy-start.1
  192.9 5.5 copy-start.2
  192.9 99.1 %all-to-all-start = ((bf16[8,2,256,2,4,128]{5,2,4,3,1,0:T(8,128)(2,1)}), bf16[8,2,256,2,4,128]{5,2,4,3,1,0:T(8,128)(2,1)}, u32[]{:S(2)}, u32[]{:S(2)}) async-start(bf16[8,2,256,2,4,128]{5,2,4,3,1,0:T(8,128)(2,1)} %copy_select_fusion), calls=%async_computation | async-start | bytes 16777216 | tf_op jit(solution)/shard_map/all_to_all | solution.py:61
  297.0 1.1 copy-start
Sparse Core Ops, SparseCore 0:
  9.5 135.2 all-gather.1
where the time goes:
time: 553 us
  blocking collectives  232 us (42%)
  waiting for transfers between devices  228 us (41%)
  matrix products  41.6 us (8%)
  local copies, waits for them, and re-layouts  20.9 us (4%)
  between operations  14.2 us (3%)
  other arithmetic  10.1 us (2%)
    unnamed x1, blocking collectives  232 us
    all_gather x1, waiting for transfers between devices, on_device(): row_block = lax.all_gather(neighbours, 'tensor', axis=0, tiled=True)  135 us
    all_to_all x1, waiting for transfers between devices, on_device(): lax.all_to_all(local_pairs, ('section', 'seq'), split_axis=0, concat_axis...  92.3 us
    dot_general x1, matrix products, on_device(): jnp.einsum('rd,kde->rke', row_block, kv_weight, preferred_element_type=jn...  28.1 us
  transfers between devices with their start and end apart: 2, of which 2 were waited for; matrix products, arithmetic and copies ran while one was open for 1% of the time, Pallas kernels for 0%

commit v1 on v0

--- a/solution.py
+++ b/solution.py
@@ -32,7 +32,21 @@
     heads_local = kv_weight.shape[2] // HD
     per_peer = PEER
     spans = slot_map.shape[0]
-    row_block = lax.all_gather(neighbours, "tensor", axis=0, tiled=True)
+    cores_n = lax.axis_size("tensor")
+    table = []
+    for nth in range(cores_n):
+        table.append((nth, (nth + 1) % cores_n))
+    nodes = []
+    for nth in range(cores_n):
+        nodes.append((nth, (nth - 1) % cores_n))
+    y1, x_next = ([neighbours], [neighbours])
+    for _ in range(cores_n // 2):
+        mixed_arr = lax.ppermute(y1[-1], axis_name="tensor", perm=table)
+        y1.append(mixed_arr)
+    for _ in range((cores_n - 1) // 2):
+        x_next.append(lax.ppermute(x_next[-1], perm=nodes, axis_name="tensor"))
+    main = jnp.concatenate([*y1[::-1], *x_next[1:]], 0)
+    row_block = jnp.roll(main, (lax.axis_index("tensor") - cores_n // 2) * neighbours.shape[0], 0)
     result = jnp.einsum("rd,kde->rke", row_block, kv_weight, preferred_element_type=jnp.float32)
     projected = result.astype(jnp.bfloat16).reshape(row_block.shape[0], 2 * kv_weight.shape[2])
     slot_values = projected.reshape(CAPC, KEYS, 2, heads_local, HD)

time: 553 us -> 710 us (1.28)
  waiting for transfers between devices: 228 us -> 299 us
  local copies, waits for them, and re-layouts: 20.9 us -> 81 us
  starting transfers between devices: 5.35 us -> 46 us
  between operations: 14.2 us -> 0.87 us
    ppermute x0 -> x15, waiting for transfers between devices: none -> 207 us  [the longest x8 207 us: on_device(): mixed_arr = lax.ppermute(y1[-1], axis_name='tensor', perm=table)]
    all_gather x1 -> x0, waiting for transfers between devices: 135 us -> none  [on_device(): row_block = lax.all_gather(neighbours, 'tensor', axis=0, tiled=True)]
    unnamed x7 -> x76, local copies, waits for them, and re-layouts: 1.66 us -> 60.5 us
    ppermute x0 -> x15, starting transfers between devices: none -> 40.7 us  [the longest x7 39 us: on_device(): x_next.append(lax.ppermute(x_next[-1], perm=nodes, axis_name='tensor'))]
  transfers between devices with their start and end apart: 2 -> 16, of which waited for: 2 -> 11; matrix products, arithmetic and copies ran while one was open for 1% -> 5% of each run, Pallas kernels for 0% -> 0%
where the time goes in v1:
time: 710 us; the launch traced here: 709 us
  waiting for transfers between devices  299 us (42%)
  blocking collectives  232 us (33%)
  local copies, waits for them, and re-layouts  81 us (11%)
  starting transfers between devices  46 us (6%)
  matrix products  39.8 us (6%)
  other arithmetic  10.2 us (1%)
    unnamed x1, blocking collectives  232 us
    ppermute x8, waiting for transfers between devices, on_device(): mixed_arr = lax.ppermute(y1[-1], axis_name='tensor', perm=table)  207 us
    all_to_all x1, waiting for transfers between devices, on_device(): lax.all_to_all(local_pairs, ('section', 'seq'), split_axis=0, concat_axis...  92.2 us
    unnamed x76, local copies, waits for them, and re-layouts  60.5 us
    ppermute x7, starting transfers between devices, on_device(): x_next.append(lax.ppermute(x_next[-1], perm=nodes, axis_name='tensor'))  39 us
    dot_general x1, matrix products, on_device(): jnp.einsum('rd,kde->rke', row_block, kv_weight, preferred_element_type=jn...  26.2 us
  transfers between devices with their start and end apart: 16, of which 11 were waited for; matrix products, arithmetic and copies ran while one was open for 5% of the time, Pallas kernels for 0%

profile of v1, /device:TPU:0, one launch (start us, length us, event | category | flops | bytes accessed | tf_op | source)
XLA Modules:
  0.0 709.4 jit_solution(7534826758015195904)
XLA Ops:
  1.7 34.0 %collective-permute-done = bf16[80,8192]{1,0:T(8,128)(2,1)S(1)} collective-permute-done((bf16[80,8192]{1,0:T(8,128)(2,1)}, bf16[80,8192]{1,0:T(8,128)(2,1)S(1)}, u32[]{:S(2)}, u32[]{:S(2)}) %collective-permute-start) | collective-permute-done | bytes 1310752 | tf_op jit(solution)/shard_map/ppermute | solution.py:44
  35.7 5.3 collective-permute-start.8
  41.0 27.9 %collective-permute-done.1 = bf16[80,8192]{1,0:T(8,128)(2,1)S(1)} collective-permute-done((bf16[80,8192]{1,0:T(8,128)(2,1)S(1)}, bf16[80,8192]{1,0:T(8,128)(2,1)S(1)}, u32[]{:S(2)}, u32[]{:S(2)}) %collective-permute-start.1) | collective-permute-done | bytes 1310752 | tf_op jit(solution)/shard_map/ppermute | solution.py:44
  70.1 5.3 collective-permute-start.9
  75.4 25.9 %collective-permute-done.2 = bf16[80,8192]{1,0:T(8,128)(2,1)S(1)} collective-permute-done((bf16[80,8192]{1,0:T(8,128)(2,1)S(1)}, bf16[80,8192]{1,0:T(8,128)(2,1)S(1)}, u32[]{:S(2)}, u32[]{:S(2)}) %collective-permute-start.2) | collective-permute-done | bytes 1310752 | tf_op jit(solution)/shard_map/ppermute | solution.py:44
  101.8 5.8 collective-permute-start.10
  107.6 25.3 %collective-permute-done.3 = bf16[80,8192]{1,0:T(8,128)(2,1)S(1)} collective-permute-done((bf16[80,8192]{1,0:T(8,128)(2,1)S(1)}, bf16[80,8192]{1,0:T(8,128)(2,1)S(1)}, u32[]{:S(2)}, u32[]{:S(2)}) %collective-permute-start.3) | collective-permute-done | bytes 1310752 | tf_op jit(solution)/shard_map/ppermute | solution.py:44
  133.0 5.8 collective-permute-start.11
  138.8 24.7 %collective-permute-done.4 = bf16[80,8192]{1,0:T(8,128)(2,1)S(1)} collective-permute-done((bf16[80,8192]{1,0:T(8,128)(2,1)S(1)}, bf16[80,8192]{1,0:T(8,128)(2,1)S(1)}, u32[]{:S(2)}, u32[]{:S(2)}) %collective-permute-start.4) | collective-permute-done | bytes 1310752 | tf_op jit(solution)/shard_map/ppermute | solution.py:44
  163.6 5.8 collective-permute-start.12
  169.4 24.2 %collective-permute-done.5 = bf16[80,8192]{1,0:T(8,128)(2,1)} collective-permute-done((bf16[80,8192]{1,0:T(8,128)(2,1)S(1)}, bf16[80,8192]{1,0:T(8,128)(2,1)}, u32[]{:S(2)}, u32[]{:S(2)}) %collective-permute-start.5) | collective-permute-done | bytes 1310752 | tf_op jit(solution)/shard_map/ppermute | solution.py:44
  194.2 5.4 collective-permute-start.13
  199.6 23.2 %collective-permute-done.6 = bf16[80,8192]{1,0:T(8,128)(2,1)} collective-permute-done((bf16[80,8192]{1,0:T(8,128)(2,1)}, bf16[80,8192]{1,0:T(8,128)(2,1)}, u32[]{:S(2)}, u32[]{:S(2)}) %collective-permute-start.6) | collective-permute-done | bytes 1310752 | tf_op jit(solution)/shard_map/ppermute | solution.py:44
  224.3 5.6 collective-permute-start.14
  229.9 21.4 %collective-permute-done.7 = bf16[80,8192]{1,0:T(8,128)(2,1)} collective-permute-done((bf16[80,8192]{1,0:T(8,128)(2,1)}, bf16[80,8192]{1,0:T(8,128)(2,1)}, u32[]{:S(2)}, u32[]{:S(2)}) %collective-permute-start.7) | collective-permute-done | bytes 1310752 | tf_op jit(solution)/shard_map/ppermute | solution.py:44
  261.1 2.5 constant_dynamic-update-slice_fusion.27
  266.1 2.7 constant_dynamic-update-slice_fusion.25
  277.1 2.5 constant_dynamic-update-slice_fusion.18
  279.6 2.5 constant_dynamic-update-slice_fusion.17
  283.2 2.5 constant_dynamic-update-slice_fusion.15
  288.2 2.5 constant_dynamic-update-slice_fusion.13
  301.3 2.6 constant_dynamic-update-slice_fusion.3
  310.2 26.2 %fusion.4 = bf16[1280,2,512]{2,0,1:T(8,128)(2,1)} fusion(bf16[2,8192,512]{2,1,0:T(8,128)(2,1)S(1)} %bitcast.44, bf16[2560,8192]{1,0:T(8,128)(2,1)} %constant_dynamic-update-slice_fusion, s32[]{:T(128)S(6)} %select_n.69), kind=kOutput, calls=%fused_computation.7 | convolution fusion | flops 21476147200 | bytes 40370180 | tf_op jit(solution)/shard_map/rd,kde->rke/dot_general | solution.py:50
  336.3 3.5 reshape_reshape.3
  339.9 8.8 %gather_fusion = bf16[16,256,2,4,128]{4,3,1,2,0:T(4,128)(2,1)} fusion(bf16[5,256,2,4,128]{4,3,1,0,2:T(4,128)(2,1)S(1)} %reshape_reshape.3, s32[1024]{0:T(1024)S(1)} %pad_clamp_fusion.1), kind=kCustom, calls=%fused_computation | custom fusion | bytes 16777280 | tf_op jit(solution)/shard_map/gather | solution.py:73
  348.7 7.8 %copy_select_fusion = bf16[8,2,256,2,4,128]{5,2,4,3,1,0:T(8,128)(2,1)} fusion(bf16[8,2,256,2,4,128]{5,4,2,3,1,0:T(4,128)(2,1)} %bitcast.41, pred[8,2]{1,0:T(8,128)(4,1)S(1)} %copy.20), kind=kLoop, calls=%fused_computation.6 | loop fusion | flops 4194304 | bytes 16777232 | tf_op jit(solution)/shard_map/jit(_where)/select_n | solution.py:72
  356.5 5.2 all-to-all-start
  363.2 92.2 %all-to-all-done = bf16[8,2,256,2,4,128]{5,2,4,3,1,0:T(8,128)(2,1)} async-done(((bf16[8,2,256,2,4,128]{5,2,4,3,1,0:T(8,128)(2,1)}), bf16[8,2,256,2,4,128]{5,2,4,3,1,0:T(8,128)(2,1)}, u32[]{:S(2)}, u32[]{:S(2)}) %all-to-all-start) | async-done | bytes 8388640 | tf_op jit(solution)/shard_map/all_to_all | solution.py:75
  455.4 4.4 gather_fusion.1
  461.9 4.1 fusion.12
  466.3 9.0 %fusion.14 = f32[320,8192]{1,0:T(8,128)} fusion(bf16[512,8192]{1,0:T(8,128)(2,1)} %param.8, bf16[40,8,4,128]{3,2,1,0:T(4,128)(2,1)S(1)} %bitcast.42), kind=kOutput, calls=%fused_computation.20 | convolution fusion | flops 2684354560 | bytes 19202048 | tf_op jit(solution)/shard_map/dot_general | solution.py:82
  475.2 232.2 %all-reduce.2 = bf16[320,8192]{1,0:T(8,128)(2,1)} all-reduce(f32[320,8192]{1,0:T(8,128)} %fusion.14), channel_id=2, replica_groups=mesh['section'=2,'seq'=4,'tensor'=16] {'tensor'}, use_global_device_ids=true, to_apply=%region_5.6.clone | all-reduce | flops 2621440 | bytes 15728640
  (106 shorter events, 51.7 us)
Async XLA Ops:
  0.0 269.9 %copy-start = (bf16[80,8192]{1,0:T(8,128)(2,1)S(1)}, bf16[80,8192]{1,0:T(8,128)(2,1)}, u32[]{:S(2)}) copy-start(bf16[80,8192]{1,0:T(8,128)(2,1)} %param.6) | copy-start | bytes 3932164
  0.0 35.7 %collective-permute-start = (bf16[80,8192]{1,0:T(8,128)(2,1)}, bf16[80,8192]{1,0:T(8,128)(2,1)S(1)}, u32[]{:S(2)}, u32[]{:S(2)}) collective-permute-start(bf16[80,8192]{1,0:T(8,128)(2,1)} %param.6), channel_id=1, source_target_pairs={{0,1},{1,2},{2,3},{3,4},{4,5},{5,6},{6,7},{7,8},{8,9},{9,10},{10,1... | collective-permute-start | bytes 3932168 | tf_op jit(solution)/shard_map/ppermute | solution.py:44
  35.7 33.3 %collective-permute-start.1 = (bf16[80,8192]{1,0:T(8,128)(2,1)S(1)}, bf16[80,8192]{1,0:T(8,128)(2,1)S(1)}, u32[]{:S(2)}, u32[]{:S(2)}) collective-permute-start(bf16[80,8192]{1,0:T(8,128)(2,1)S(1)} %collective-permute-done), channel_id=1, source_target_pairs={{0,1},{1,2},{2,3},{3,4},{4,5},{5,6},{6,7},{7,8},{8,9},{9,10},{10,1... | collective-permute-start | bytes 3932168 | tf_op jit(solution)/shard_map/ppermute | solution.py:44
  35.7 33.3 %collective-permute-start.8 = (bf16[80,8192]{1,0:T(8,128)(2,1)}, bf16[80,8192]{1,0:T(8,128)(2,1)S(1)}, u32[]{:S(2)}, u32[]{:S(2)}) collective-permute-start(bf16[80,8192]{1,0:T(8,128)(2,1)} %param.6), channel_id=1, source_target_pairs={{0,15},{1,0},{2,1},{3,2},{4,3},{5,4},{6,5},{7,6},{8,7},{9,8},{10,9... | collective-permute-start | bytes 3932168 | tf_op jit(solution)/shard_map/ppermute | solution.py:47
  68.9 32.8 %copy-start.3 = (bf16[80,8192]{1,0:T(8,128)(2,1)}, bf16[80,8192]{1,0:T(8,128)(2,1)S(1)}, u32[]{:S(2)}) copy-start(bf16[80,8192]{1,0:T(8,128)(2,1)S(1)} %collective-permute-done.1) | copy-start | bytes 3932164
  68.9 32.4 %collective-permute-start.2 = (bf16[80,8192]{1,0:T(8,128)(2,1)S(1)}, bf16[80,8192]{1,0:T(8,128)(2,1)S(1)}, u32[]{:S(2)}, u32[]{:S(2)}) collective-permute-start(bf16[80,8192]{1,0:T(8,128)(2,1)S(1)} %collective-permute-done.1), channel_id=1, source_target_pairs={{0,1},{1,2},{2,3},{3,4},{4,5},{5,6},{6,7},{7,8},{8,9},{9,10},{10,1... | collective-permute-start | bytes 3932168 | tf_op jit(solution)/shard_map/ppermute | solution.py:44
  70.1 31.6 %collective-permute-start.9 = (bf16[80,8192]{1,0:T(8,128)(2,1)S(1)}, bf16[80,8192]{1,0:T(8,128)(2,1)S(1)}, u32[]{:S(2)}, u32[]{:S(2)}) collective-permute-start(bf16[80,8192]{1,0:T(8,128)(2,1)S(1)} %collective-permute-done.8), channel_id=1, source_target_pairs={{0,15},{1,0},{2,1},{3,2},{4,3},{5,4},{6,5},{7,6},{8,7},{9,8},{10,9... | collective-permute-start | bytes 3932168 | tf_op jit(solution)/shard_map/ppermute | solution.py:47
  101.3 31.7 %copy-start.7 = (bf16[80,8192]{1,0:T(8,128)(2,1)}, bf16[80,8192]{1,0:T(8,128)(2,1)S(1)}, u32[]{:S(2)}) copy-start(bf16[80,8192]{1,0:T(8,128)(2,1)S(1)} %collective-permute-done.2) | copy-start | bytes 3932164
  101.3 31.5 %collective-permute-start.3 = (bf16[80,8192]{1,0:T(8,128)(2,1)S(1)}, bf16[80,8192]{1,0:T(8,128)(2,1)S(1)}, u32[]{:S(2)}, u32[]{:S(2)}) collective-permute-start(bf16[80,8192]{1,0:T(8,128)(2,1)S(1)} %collective-permute-done.2), channel_id=1, source_target_pairs={{0,1},{1,2},{2,3},{3,4},{4,5},{5,6},{6,7},{7,8},{8,9},{9,10},{10,1... | collective-permute-start | bytes 3932168 | tf_op jit(solution)/shard_map/ppermute | solution.py:44
  101.8 31.3 %collective-permute-start.10 = (bf16[80,8192]{1,0:T(8,128)(2,1)S(1)}, bf16[80,8192]{1,0:T(8,128)(2,1)S(1)}, u32[]{:S(2)}, u32[]{:S(2)}) collective-permute-start(bf16[80,8192]{1,0:T(8,128)(2,1)S(1)} %collective-permute-done.9), channel_id=1, source_target_pairs={{0,15},{1,0},{2,1},{3,2},{4,3},{5,4},{6,5},{7,6},{8,7},{9,8},{10,9... | collective-permute-start | bytes 3932168 | tf_op jit(solution)/shard_map/ppermute | solution.py:47
  132.9 30.7 %copy-start.11 = (bf16[80,8192]{1,0:T(8,128)(2,1)}, bf16[80,8192]{1,0:T(8,128)(2,1)S(1)}, u32[]{:S(2)}) copy-start(bf16[80,8192]{1,0:T(8,128)(2,1)S(1)} %collective-permute-done.3) | copy-start | bytes 3932164
  132.9 30.7 %collective-permute-start.4 = (bf16[80,8192]{1,0:T(8,128)(2,1)S(1)}, bf16[80,8192]{1,0:T(8,128)(2,1)S(1)}, u32[]{:S(2)}, u32[]{:S(2)}) collective-permute-start(bf16[80,8192]{1,0:T(8,128)(2,1)S(1)} %collective-permute-done.3), channel_id=1, source_target_pairs={{0,1},{1,2},{2,3},{3,4},{4,5},{5,6},{6,7},{7,8},{8,9},{9,10},{10,1... | collective-permute-start | bytes 3932168 | tf_op jit(solution)/shard_map/ppermute | solution.py:44
  133.0 30.6 %collective-permute-start.11 = (bf16[80,8192]{1,0:T(8,128)(2,1)S(1)}, bf16[80,8192]{1,0:T(8,128)(2,1)}, u32[]{:S(2)}, u32[]{:S(2)}) collective-permute-start(bf16[80,8192]{1,0:T(8,128)(2,1)S(1)} %collective-permute-done.10), channel_id=1, source_target_pairs={{0,15},{1,0},{2,1},{3,2},{4,3},{5,4},{6,5},{7,6},{8,7},{9,8},{10,9... | collective-permute-start | bytes 3932168 | tf_op jit(solution)/shard_map/ppermute | solution.py:47
  163.6 29.9 %collective-permute-start.5 = (bf16[80,8192]{1,0:T(8,128)(2,1)S(1)}, bf16[80,8192]{1,0:T(8,128)(2,1)}, u32[]{:S(2)}, u32[]{:S(2)}) collective-permute-start(bf16[80,8192]{1,0:T(8,128)(2,1)S(1)} %collective-permute-done.4), channel_id=1, source_target_pairs={{0,1},{1,2},{2,3},{3,4},{4,5},{5,6},{6,7},{7,8},{8,9},{9,10},{10,1... | collective-permute-start | bytes 3932168 | tf_op jit(solution)/shard_map/ppermute | solution.py:44
  163.6 30.6 %collective-permute-start.12 = (bf16[80,8192]{1,0:T(8,128)(2,1)}, bf16[80,8192]{1,0:T(8,128)(2,1)}, u32[]{:S(2)}, u32[]{:S(2)}) collective-permute-start(bf16[80,8192]{1,0:T(8,128)(2,1)} %collective-permute-done.11), channel_id=1, source_target_pairs={{0,15},{1,0},{2,1},{3,2},{4,3},{5,4},{6,5},{7,6},{8,7},{9,8},{10,9... | collective-permute-start | bytes 3932168 | tf_op jit(solution)/shard_map/ppermute | solution.py:47
  193.5 29.3 %collective-permute-start.6 = (bf16[80,8192]{1,0:T(8,128)(2,1)}, bf16[80,8192]{1,0:T(8,128)(2,1)}, u32[]{:S(2)}, u32[]{:S(2)}) collective-permute-start(bf16[80,8192]{1,0:T(8,128)(2,1)} %collective-permute-done.5), channel_id=1, source_target_pairs={{0,1},{1,2},{2,3},{3,4},{4,5},{5,6},{6,7},{7,8},{8,9},{9,10},{10,1... | collective-permute-start | bytes 3932168 | tf_op jit(solution)/shard_map/ppermute | solution.py:44
  194.2 30.1 %collective-permute-start.13 = (bf16[80,8192]{1,0:T(8,128)(2,1)}, bf16[80,8192]{1,0:T(8,128)(2,1)}, u32[]{:S(2)}, u32[]{:S(2)}) collective-permute-start(bf16[80,8192]{1,0:T(8,128)(2,1)} %collective-permute-done.12), channel_id=1, source_target_pairs={{0,15},{1,0},{2,1},{3,2},{4,3},{5,4},{6,5},{7,6},{8,7},{9,8},{10,9... | collective-permute-start | bytes 3932168 | tf_op jit(solution)/shard_map/ppermute | solution.py:47
  222.8 28.4 %collective-permute-start.7 = (bf16[80,8192]{1,0:T(8,128)(2,1)}, bf16[80,8192]{1,0:T(8,128)(2,1)}, u32[]{:S(2)}, u32[]{:S(2)}) collective-permute-start(bf16[80,8192]{1,0:T(8,128)(2,1)} %collective-permute-done.6), channel_id=1, source_target_pairs={{0,1},{1,2},{2,3},{3,4},{4,5},{5,6},{6,7},{7,8},{8,9},{9,10},{10,1... | collective-permute-start | bytes 3932168 | tf_op jit(solution)/shard_map/ppermute | solution.py:44
  224.3 46.8 %copy-start.2 = (bf16[80,8192]{1,0:T(8,128)(2,1)S(1)}, bf16[80,8192]{1,0:T(8,128)(2,1)}, u32[]{:S(2)}) copy-start(bf16[80,8192]{1,0:T(8,128)(2,1)} %copy-done.1) | copy-start | bytes 3932164
  224.3 48.0 %copy-start.6 = (bf16[80,8192]{1,0:T(8,128)(2,1)S(1)}, bf16[80,8192]{1,0:T(8,128)(2,1)}, u32[]{:S(2)}) copy-start(bf16[80,8192]{1,0:T(8,128)(2,1)} %copy-done.5) | copy-start | bytes 3932164
  224.3 49.2 %copy-start.10 = (bf16[80,8192]{1,0:T(8,128)(2,1)S(1)}, bf16[80,8192]{1,0:T(8,128)(2,1)}, u32[]{:S(2)}) copy-start(bf16[80,8192]{1,0:T(8,128)(2,1)} %copy-done.9) | copy-start | bytes 3932164
  224.3 57.8 %collective-permute-start.14 = (bf16[80,8192]{1,0:T(8,128)(2,1)}, bf16[80,8192]{1,0:T(8,128)(2,1)S(1)}, u32[]{:S(2)}, u32[]{:S(2)}) collective-permute-start(bf16[80,8192]{1,0:T(8,128)(2,1)} %collective-permute-done.13), channel_id=1, source_target_pairs={{0,15},{1,0},{2,1},{3,2},{4,3},{5,4},{6,5},{7,6},{8,7},{9,8},{10,9... | collective-permute-start | bytes 3932168 | tf_op jit(solution)/shard_map/ppermute | solution.py:47
  266.1 24.6 %copy-start.14 = (bf16[80,8192]{1,0:T(8,128)(2,1)S(1)}, bf16[80,8192]{1,0:T(8,128)(2,1)}, u32[]{:S(2)}) copy-start(bf16[80,8192]{1,0:T(8,128)(2,1)} %copy-done.13) | copy-start | bytes 3932164
  268.7 23.2 %copy-start.12 = (bf16[80,8192]{1,0:T(8,128)(2,1)S(1)}, bf16[80,8192]{1,0:T(8,128)(2,1)}, u32[]{:S(2)}) copy-start(bf16[80,8192]{1,0:T(8,128)(2,1)} %copy-done.11) | copy-start | bytes 3932164
  269.9 23.2 %copy-start.8 = (bf16[80,8192]{1,0:T(8,128)(2,1)S(1)}, bf16[80,8192]{1,0:T(8,128)(2,1)}, u32[]{:S(2)}) copy-start(bf16[80,8192]{1,0:T(8,128)(2,1)} %copy-done.7) | copy-start | bytes 3932164
  271.0 23.2 %copy-start.4 = (bf16[80,8192]{1,0:T(8,128)(2,1)S(1)}, bf16[80,8192]{1,0:T(8,128)(2,1)}, u32[]{:S(2)}) copy-start(bf16[80,8192]{1,0:T(8,128)(2,1)} %copy-done.3) | copy-start | bytes 3932164
  290.7 19.5 %slice-start = ((s8[16777216]{0:T(1024)(128)(4,1)}), s8[4194304]{0:T(1024)(128)(4,1)S(1)}, s32[]{:S(2)}) async-start(s8[16777216]{0:T(1024)(128)(4,1)} %bitcast.43), calls=%async_computation.1 | async-start | bytes 8388608
  294.3 15.9 %slice-start.1 = ((s8[16777216]{0:T(1024)(128)(4,1)}), s8[4194304]{0:T(1024)(128)(4,1)S(1)}, s32[]{:S(2)}) async-start(s8[16777216]{0:T(1024)(128)(4,1)} %bitcast.43), calls=%async_computation.2 | async-start | bytes 8388608
  297.8 12.3 %slice-start.2 = ((s8[16777216]{0:T(1024)(128)(4,1)}), s8[4194304]{0:T(1024)(128)(4,1)S(1)}, s32[]{:S(2)}) async-start(s8[16777216]{0:T(1024)(128)(4,1)} %bitcast.43), calls=%async_computation.3 | async-start | bytes 8388608
  348.7 13.1 %copy-start.16 = (bf16[320,512]{1,0:T(8,128)(2,1)S(1)}, bf16[320,512]{1,0:T(8,128)(2,1)}, u32[]{:S(2)}) copy-start(bf16[320,512]{1,0:T(8,128)(2,1)} %param.5) | copy-start | bytes 983044
  348.7 13.2 %copy-start.17 = (u32[128]{0:T(128)S(1)}, u32[128]{0:T(128)}, u32[]{:S(2)}) copy-start(u32[128]{0:T(128)} %constant.86) | copy-start | bytes 1540
  356.5 98.9 %all-to-all-start = ((bf16[8,2,256,2,4,128]{5,2,4,3,1,0:T(8,128)(2,1)}), bf16[8,2,256,2,4,128]{5,2,4,3,1,0:T(8,128)(2,1)}, u32[]{:S(2)}, u32[]{:S(2)}) async-start(bf16[8,2,256,2,4,128]{5,2,4,3,1,0:T(8,128)(2,1)} %copy_select_fusion), calls=%async_computation | async-start | bytes 16777216 | tf_op jit(solution)/shard_map/all_to_all | solution.py:75
  (6 other events, 28.5 us)
